TPU v7x, 512 devices: a whole 4x8x8 slice. The times are simulated.
512 devices in a mesh: segment: 4 (over z_lo), seq: 16 (over z_hi, x, core), mp: 8 (over y).
Axes of the slice: x: 4, y: 8, z: 8 (z_hi: 2, z_lo: 4; z = z_hi * 4 + z_lo), core: 2. Of those that a mesh axis runs over, the one named last changes fastest.
Arguments:
- latents: bfloat16 [4, 16, 256, 4096], P('segment', 'seq', None, 'mp'), may hold values from -6 to 6
- w_qkv: bfloat16 [4, 4096, 3, 4096], P('segment', 'seq', None, 'mp'), may hold values from -1 to 1
- w_out: bfloat16 [4, 4096, 4096], P('segment', 'mp', 'seq'), may hold values from -0.09375 to 0.09375
- mod_shift: float32 [4, 4096], P('segment'), may hold values from -3 to 3
- mod_scale: float32 [4, 4096], P('segment'), may hold values from 0.1 to 1.9
- mod_gate: float32 [4, 4096], P('segment'), may hold values from 0.5 to 1.5
- counts: int32 [4, 16], P('segment'), may hold values from 64 to 256, as said below
Outputs:
- next_latents: bfloat16 [4, 16, 256, 4096], P('segment', 'seq', None, 'mp')
Inputs may be any that keep to these rules, and one draw needn't show every extreme that they name: `counts`: in every section's clip at least one frame has all 256 patch positions valid.
All inputs are finite; a program needn't handle non-finite values.
Results may differ from a plain program's by a relative error of at most 0.01.
Values may be sent and summed in bfloat16 or wider, within the bound.
No kernel may reach another device: no remote copies, remote signals or barrier semaphores. Data moves between devices by JAX's collectives and lax.ppermute only.
A program may use at most 64 MiB of HBM per device.

v0:
```python
import math
import jax
import jax.numpy as jnp
from jax import lax
from jax.sharding import PartitionSpec as P

HD = 128
EPS = 1e-06
NEG_FILL = -1e30


def passed_along(x, axis, by):
    length = lax.axis_size(axis)
    return lax.ppermute(x, axis, [(i, (i + by) % length) for i in range(length)])


def masked_attention(queries, keys_in, values, usable):
    factor = 1.0 / math.sqrt(queries.shape[-1])
    scores = (
        jnp.einsum("...ihe,...jhe->...hij", queries, keys_in, preferred_element_type=jnp.float32)
        * factor
    )
    allowed = usable[..., None, :, None] & usable[..., None, None, :]
    masked = jnp.where(allowed, scores, NEG_FILL)
    highest = jnp.max(masked, axis=-1, keepdims=True)
    raised = jnp.where(allowed, jnp.exp(masked - highest), 0.0)
    spare_one = jnp.where(usable, 0.0, 1.0)[..., None, :, None]
    weights = (raised / (jnp.sum(raised, axis=-1, keepdims=True) + spare_one)).astype(jnp.bfloat16)
    blended = jnp.einsum(
        "...hij,...jhe->...ihe", weights, values, preferred_element_type=jnp.float32
    )
    return blended.astype(jnp.bfloat16)


SEQ = ("zh", "x", "c")


def seq_index():
    return (lax.axis_index("zh") * lax.axis_size("x") + lax.axis_index("x")) * lax.axis_size(
        "c"
    ) + lax.axis_index("c")


def gather_seq(block):
    across = lax.all_gather(block, "zh", axis=0)
    along = lax.all_gather(across, "x", axis=1)
    both = lax.all_gather(along, "c", axis=2)
    return both.reshape((-1,) + block.shape[1:])


def relay_features(rows_now):
    return lax.all_to_all(rows_now, SEQ, split_axis=0, concat_axis=0, tiled=True)


def pass_onward(rows_now):
    return passed_along(rows_now, "segment", 1)


def on_device(latents, w_qkv, w_out, mod_shift, mod_scale, mod_gate, counts):
    frames = lax.axis_size(SEQ)
    patches = latents.shape[2]
    narrow = latents.shape[3]
    span = patches // frames
    segment_rows = latents[0, 0]
    gathered = lax.all_gather(latents, "mp", axis=3, tiled=True)[0, 0]
    widened = gathered.astype(jnp.float32)
    average = jnp.mean(widened, axis=-1, keepdims=True)
    centred = widened - average
    variance = jnp.mean(centred * centred, axis=-1, keepdims=True)
    modulated = (centred * lax.rsqrt(variance + EPS) * mod_scale[0] + mod_shift[0]).astype(
        jnp.bfloat16
    )
    columns = w_qkv.shape[2] * w_qkv.shape[3]
    piece = gather_seq(w_qkv[0])
    height = piece.shape[0]
    projected = jnp.dot(
        modulated, piece.reshape(height, columns), preferred_element_type=jnp.float32
    )
    local_heads = w_qkv.shape[3] // HD
    projected = projected.astype(jnp.bfloat16).reshape(patches, 3, local_heads, HD)
    frame_here = seq_index()
    clip_counts = counts[0]
    positions = jnp.arange(frames)

    def spatial(triple):
        count_here = jnp.sum(jnp.where(positions == frame_here, clip_counts, 0))
        usable = jnp.arange(patches) < count_here
        return masked_attention(triple[:, 0], triple[:, 1], triple[:, 2], usable)

    def temporal(triple):
        by_place = triple.reshape(frames, span, 3, local_heads, HD).transpose(1, 0, 2, 3, 4)
        location = frame_here * span + jnp.arange(span)
        usable = location[:, None] < clip_counts[None, :]
        blended = masked_attention(by_place[:, :, 0], by_place[:, :, 1], by_place[:, :, 2], usable)
        return blended.transpose(1, 0, 2, 3).reshape(patches, local_heads, HD)

    attended = lax.cond(lax.axis_index("segment") % 2 == 0, spatial, temporal, projected)
    attended = attended.reshape(patches, local_heads * HD)
    out_blocks = gather_seq(w_out[0][None])
    member = lax.axis_index("mp")
    partials = jnp.einsum(
        "tr,brc->tbc", attended, out_blocks, preferred_element_type=jnp.float32
    ).reshape(patches, -1)
    summed = lax.psum_scatter(
        partials.astype(jnp.bfloat16), "mp", scatter_dimension=1, tiled=True
    ).astype(jnp.float32)
    gate_here = lax.dynamic_slice_in_dim(mod_gate[0], member * narrow, narrow)
    updated = (segment_rows.astype(jnp.float32) + gate_here * summed).astype(jnp.bfloat16)
    updated = updated.reshape(frames, span, narrow)
    moved = pass_onward(relay_features(updated))
    return moved.reshape(1, 1, patches, narrow)


def solution(mesh):
    seg, seq, mp = mesh.devices.shape
    inner = mesh.devices.reshape(seg, 2, seq // 4, 2, mp)
    fine = jax.sharding.Mesh(inner, ("segment", "zh", "x", "c", "mp"))
    return jax.shard_map(
        on_device,
        mesh=fine,
        in_specs=(
            P("segment", SEQ, None, "mp"),
            P("segment", SEQ, None, "mp"),
            P("segment", "mp", SEQ),
            P("segment", None),
            P("segment", None),
            P("segment", None),
            P("segment", None),
        ),
        out_specs=P("segment", SEQ, None, "mp"),
        check_vma=False,
    )
```

profile of v0, /device:TPU:1, one launch (start us, length us, event | category | flops | bytes accessed | tf_op | source)
XLA Modules:
  0.0 409.4 jit_solution(5378004970461024760)
XLA Ops:
  6.5 0.7 all-gather.14.cloned.1.call-update
  7.3 19.6 %all-gather.2 = bf16[2,512,256]{2,1,0:T(8,128)(2,1)} all-gather(bf16[1,512,256]{2,1,0:T(8,128)(2,1)} %param.11), channel_id=4, replica_groups=mesh['segment'=4,'zh'=2,'x'=4,'c'=2,'mp'=8] {'zh'}, dimensions={0}, use_global_device_ids=true | all-gather | bytes 786432 | tf_op jit(solution)/shard_map/all_gather | solution.py:45
  26.9 44.4 %all-gather.14.cloned.1.call-done = bf16[2,256,3,512]{3,1,2,0:T(8,128)(2,1)} async-done(((bf16[1,256,3,512]{3,1,2,0:T(8,128)(2,1)}), bf16[2,256,3,512]{3,1,2,0:T(8,128)(2,1)}) %all-gather.14.cloned.1.call-update) | async-done | bytes 1572880 | tf_op jit(solution)/shard_map/all_gather | solution.py:45
  72.0 34.1 %all-gather.20.cloned.1.call-done = bf16[2,2048,256]{2,1,0:T(8,128)(2,1)} async-done(((bf16[2,512,256]{2,1,0:T(8,128)(2,1)}), bf16[2,2048,256]{2,1,0:T(8,128)(2,1)}) %all-gather.20.cloned.1.call-update) | async-done | bytes 2097168 | tf_op jit(solution)/shard_map/all_gather | solution.py:46
  106.2 73.1 %all-gather.16.cloned.1.call-done = bf16[2,1024,3,512]{3,1,2,0:T(8,128)(2,1)} async-done(((bf16[2,256,3,512]{3,1,2,0:T(8,128)(2,1)}), bf16[2,1024,3,512]{3,1,2,0:T(8,128)(2,1)}) %all-gather.16.cloned.1.call-update) | async-done | bytes 6291472 | tf_op jit(solution)/shard_map/all_gather | solution.py:46
  179.3 11.4 %copy.28 = bf16[2,4,256,3,512]{2,1,0,4,3:T(4,128)(2,1)} copy(bf16[2,4,256,3,512]{4,2,1,3,0:T(8,128)(2,1)} %bitcast.90) | data formatting | bytes 12582912 | tf_op jit(solution)/shard_map/all_gather | solution.py:46
  190.8 30.5 %all-gather.12.cloned.1.call-done = bf16[1,1,256,4096]{3,2,1,0:T(8,128)(2,1)} async-done(((bf16[1,1,256,512]{3,2,1,0:T(8,128)(2,1)}), bf16[1,1,256,4096]{3,2,1,0:T(8,128)(2,1)}) %all-gather.12.cloned.1.call-update) | async-done | bytes 2097168 | tf_op jit(solution)/shard_map/all_gather | solution.py:65
  221.4 2.0 convert_reduce_fusion
  223.3 2.3 fusion.30
  225.6 23.9 %all-gather.22.cloned.1.call-done = bf16[2,4,2,512,256]{4,3,2,1,0:T(8,128)(2,1)} async-done(((bf16[2,4,1,512,256]{4,3,2,1,0:T(8,128)(2,1)}), bf16[2,4,2,512,256]{4,3,2,1,0:T(8,128)(2,1)}) %all-gather.22.cloned.1.call-update) | async-done | bytes 4194320 | tf_op jit(solution)/shard_map/all_gather | solution.py:47
  249.5 6.4 %copy.30 = bf16[16,256,512]{2,1,0:T(8,128)(2,1)} copy(bf16[16,256,512]{1,2,0:T(8,128)(2,1)} %bitcast.91) | data formatting | bytes 8388608 | tf_op jit(solution)/shard_map/tr,brc->tbc/dot_general | solution.py:101
  255.9 29.7 %all-gather.18.cloned.1.call-done = bf16[2,4,512,3,512]{2,1,0,4,3:T(4,128)(2,1)} async-done(((bf16[2,4,256,3,512]{2,1,0,4,3:T(4,128)(2,1)}), bf16[2,4,512,3,512]{2,1,0,4,3:T(4,128)(2,1)}) %all-gather.18.cloned.1.call-update) | async-done | bytes 12582928 | tf_op jit(solution)/shard_map/all_gather | solution.py:47
  285.6 21.0 %reshape_reshape.6 = bf16[4096,1536]{0,1:T(8,128)(2,1)} reshape(bf16[2,4,512,3,512]{2,1,0,4,3:T(4,128)(2,1)} %all-gather.18.cloned.1.call-done) | data formatting | bytes 25165824 | tf_op jit(solution)/shard_map/reshape;reshape | solution.py:77
  306.6 8.1 %convolution_convert_fusion.3 = bf16[256,1536]{1,0:T(8,128)(2,1)S(1)} fusion(bf16[4096,1536]{0,1:T(8,128)(2,1)} %reshape_reshape.6, bf16[1,1,256,4096]{3,2,1,0:T(8,128)(2,1)S(1)} %copy-done.1, f32[4096]{0:T(1024)S(1)} %bitcast.105, f32[4096]{0:T(1024)S(1)} %bitcast.106, f32[256]{0:T(256)S(1)} %add_rsqrt_fusion, f32[256]{0:T(256)S(1)} %broadcast_multiply_fusion), kind=kOutput, calls=%fused_computation.57 | convolution fusion | flops 3227910144 | bytes 15501312 | tf_op jit(solution)/shard_map/dot_general | solution.py:76
  314.7 4.0 conditional.1
  314.8 0.7 fusion.14
  317.9 0.8 convolution_convert_fusion.1
  318.7 4.9 %convolution_convert_fusion.2 = bf16[256,4096]{1,0:T(8,128)(2,1)} fusion(bf16[256,512]{0,1:T(8,128)(2,1)S(1)} %get-tuple-element.40, bf16[4096,512]{1,0:T(8,128)(2,1)} %bitcast.89), kind=kOutput, calls=%fused_computation.49 | convolution fusion | flops 1074790400 | bytes 6553600 | tf_op jit(solution)/shard_map/tr,brc->tbc/dot_general | solution.py:101
  323.7 40.9 %reduce-scatter.2.cloned.1.call-done = bf16[256,512]{1,0:T(8,128)(2,1)} async-done(((bf16[256,4096]{1,0:T(8,128)(2,1)}), bf16[256,512]{1,0:T(8,128)(2,1)}) %reduce-scatter.2.cloned.1.call-update) | async-done | bytes 262160 | tf_op jit(solution)/shard_map/reduce_scatter | solution.py:104
  364.5 1.0 fusion.37
  365.6 25.7 %all_to_all.5 = bf16[16,16,512]{2,1,0:T(8,128)(2,1)S(1)} all-to-all(bf16[16,16,512]{2,1,0:T(8,128)(2,1)S(1)} %bitcast.93), channel_id=1, replica_groups=mesh['segment'=4,'zh'=2,'x'=4,'c'=2,'mp'=8] {'zh','x','c'}, dimensions={0} | all-to-all | bytes 524288 | tf_op jit(solution)/shard_map/all_to_all | solution.py:52
  391.2 4.9 %collective-permute-start = (bf16[16,16,512]{2,1,0:T(8,128)(2,1)S(1)}, bf16[16,16,512]{2,1,0:T(8,128)(2,1)S(1)}, u32[]{:S(2)}, u32[]{:S(2)}) collective-permute-start(bf16[16,16,512]{2,1,0:T(8,128)(2,1)S(1)} %all_to_all.5), channel_id=1, source_target_pairs={{0,128},{128,256},{256,384},{384,0},{1,129},{129,257},{257,385},{3... | collective-permute-start | bytes 786440 | tf_op jit(solution)/shard_map/ppermute | solution.py:14
  396.2 5.6 %collective-permute-done = bf16[16,16,512]{2,1,0:T(8,128)(2,1)S(1)} collective-permute-done((bf16[16,16,512]{2,1,0:T(8,128)(2,1)S(1)}, bf16[16,16,512]{2,1,0:T(8,128)(2,1)S(1)}, u32[]{:S(2)}, u32[]{:S(2)}) %collective-permute-start) | collective-permute-done | bytes 262176 | tf_op jit(solution)/shard_map/ppermute | solution.py:14
  401.8 0.7 copy.43
  (35 shorter events, 3.3 us)
Async XLA Ops:
  6.5 317.1 %copy-start = (f32[1,4096]{1,0:T(1,128)S(1)}, f32[1,4096]{1,0:T(1,128)}, u32[]{:S(2)}) copy-start(f32[1,4096]{1,0:T(1,128)} %param.14) | copy-start | bytes 49156
  6.5 64.8 %all-gather.14.cloned.1.call-start = ((), (), s32[]{:S(2)}) async-start(), calls=%async_computation.3 | async-start | bytes 2359296 | tf_op jit(solution)/shard_map/all_gather | solution.py:45
  7.3 98.9 %all-gather.20.cloned.1.call-start = ((), (), s32[]{:S(2)}) async-start(), calls=%async_computation.7 | async-start | bytes 2621440 | tf_op jit(solution)/shard_map/all_gather | solution.py:46
  26.9 152.4 %all-gather.16.cloned.1.call-start = ((), (), s32[]{:S(2)}) async-start(), calls=%async_computation.5 | async-start | bytes 7864320 | tf_op jit(solution)/shard_map/all_gather | solution.py:46
  71.4 150.0 %all-gather.12.cloned.1.call-start = ((), (), s32[]{:S(2)}) async-start(), calls=%async_computation.2 | async-start | bytes 2359296 | tf_op jit(solution)/shard_map/all_gather | solution.py:65
  72.0 177.5 %all-gather.22.cloned.1.call-start = ((), (), s32[]{:S(2)}) async-start(), calls=%async_computation.8 | async-start | bytes 6291456 | tf_op jit(solution)/shard_map/all_gather | solution.py:47
  106.2 179.4 %all-gather.18.cloned.1.call-start = ((), (), s32[]{:S(2)}) async-start(), calls=%async_computation.6 | async-start | bytes 18874368 | tf_op jit(solution)/shard_map/all_gather | solution.py:47
  190.8 173.8 %reduce-scatter.2.cloned.1.call-start = ((), (), s32[]{:S(2)}) async-start(), calls=%async_computation.4 | async-start | bytes 2359296 | tf_op jit(solution)/shard_map/reduce_scatter | solution.py:104
  255.9 50.7 %copy-start.1 = (bf16[1,1,256,4096]{3,2,1,0:T(8,128)(2,1)S(1)}, bf16[1,1,256,4096]{3,2,1,0:T(8,128)(2,1)}, u32[]{:S(2)}) copy-start(bf16[1,1,256,4096]{3,2,1,0:T(8,128)(2,1)} %all-gather.12.cloned.1.call-done) | copy-start | bytes 6291460
  255.9 50.7 %copy-start.4 = (f32[1,4096]{1,0:T(1,128)S(1)}, f32[1,4096]{1,0:T(1,128)}, u32[]{:S(2)}) copy-start(f32[1,4096]{1,0:T(1,128)} %param.12) | copy-start | bytes 49156
  255.9 50.7 %copy-start.5 = (f32[1,4096]{1,0:T(1,128)S(1)}, f32[1,4096]{1,0:T(1,128)}, u32[]{:S(2)}) copy-start(f32[1,4096]{1,0:T(1,128)} %param.13) | copy-start | bytes 49156
  306.6 8.1 %copy-start.3 = (s32[1,16]{1,0:T(1,128)S(1)}, s32[1,16]{1,0:T(1,128)}, u32[]{:S(2)}) copy-start(s32[1,16]{1,0:T(1,128)} %param.15) | copy-start | bytes 196
  318.7 45.8 %copy-start.2 = (bf16[1,1,256,512]{3,2,1,0:T(8,128)(2,1)S(1)}, bf16[1,1,256,512]{3,2,1,0:T(8,128)(2,1)}, u32[]{:S(2)}) copy-start(bf16[1,1,256,512]{3,2,1,0:T(8,128)(2,1)} %param.9) | copy-start | bytes 786436
  391.2 10.6 %collective-permute-start = (bf16[16,16,512]{2,1,0:T(8,128)(2,1)S(1)}, bf16[16,16,512]{2,1,0:T(8,128)(2,1)S(1)}, u32[]{:S(2)}, u32[]{:S(2)}) collective-permute-start(bf16[16,16,512]{2,1,0:T(8,128)(2,1)S(1)} %all_to_all.5), channel_id=1, source_target_pairs={{0,128},{128,256},{256,384},{384,0},{1,129},{129,257},{257,385},{3... | collective-permute-start | bytes 786440 | tf_op jit(solution)/shard_map/ppermute | solution.py:14
Sparse Core Ops, SparseCore 0:
  9.4 61.9 all-gather.13
  73.5 32.6 all-gather.19
  108.2 71.0 all-gather.15
  181.3 40.0 all-gather.11
  223.3 26.1 all-gather.21
  251.5 34.0 all-gather.17
  323.8 40.7 reduce-scatter.1
where the time goes:
time: 411 us; the launch traced here: 409 us
  waiting for transfers between devices  284 us (69%)
  blocking collectives  45.2 us (11%)
  local copies, waits for them, and re-layouts  39.8 us (10%)
  matrix products  14.4 us (4%)
  between operations  13.6 us (3%)
  other arithmetic  7.48 us (2%)
  starting transfers between devices  5.16 us (1%)
    all_gather x2, waiting for transfers between devices, gather_seq(): along = lax.all_gather(across, 'x', axis=1)  107 us
    all_gather x2, waiting for transfers between devices, gather_seq(): both = lax.all_gather(along, 'c', axis=2)  53.6 us
    all_gather x1, waiting for transfers between devices, gather_seq(): across = lax.all_gather(block, 'zh', axis=0)  44.4 us
    reduce_scatter x1, waiting for transfers between devices, on_device(): lax.psum_scatter(partials.astype(jnp.bfloat16), 'mp', scatter_dimension=1...  40.9 us
    all_gather x1, waiting for transfers between devices, on_device(): gathered = lax.all_gather(latents, 'mp', axis=3, tiled=True)[0, 0]  30.5 us
    all_to_all x1, blocking collectives, relay_features(): lax.all_to_all(rows_now, SEQ, split_axis=0, concat_axis=0, tiled=True)  25.7 us
    another operation x1, local copies, waits for them, and re-layouts, on_device(): piece.reshape(height, columns)  21 us
    all_gather x1, blocking collectives, gather_seq(): across = lax.all_gather(block, 'zh', axis=0)  19.6 us
  transfers between devices with their start and end apart: 8, of which 8 were waited for; matrix products, arithmetic and copies ran while one was open for 5% of the time, Pallas kernels for 0%

commit v1 on v0

--- a/solution.py
+++ b/solution.py
@@ -7,6 +7,28 @@
 HD = 128
 EPS = 1e-06
 NEG_FILL = -1e30
+
+
+def joined_along(blocks, dim):
+    blocks = jnp.moveaxis(blocks, 0, dim)
+    lengths = blocks.shape
+    return blocks.reshape(*lengths[:dim], lengths[dim] * lengths[dim + 1], *lengths[dim + 2 :])
+
+
+def collect(shard, axis, dim):
+    length = lax.axis_size(axis)
+    pairs = [(i, (i + 1) % length) for i in range(length)]
+    back = [(b, a) for a, b in pairs]
+    lower, upper = ([], [])
+    for turn in range(length - 1):
+        if turn % 2 == 0:
+            lower.append(lax.ppermute(lower[-1] if lower else shard, axis, pairs))
+        else:
+            upper.append(lax.ppermute(upper[-1] if upper else shard, axis, back))
+    parts = jnp.stack([*lower[::-1], shard, *upper])
+    shift = lax.axis_index(axis) - len(lower)
+    parts = parts[(jnp.arange(length) - shift) % length]
+    return joined_along(parts, dim)
 
 
 def passed_along(x, axis, by):
@@ -62,7 +84,7 @@
     narrow = latents.shape[3]
     span = patches // frames
     segment_rows = latents[0, 0]
-    gathered = lax.all_gather(latents, "mp", axis=3, tiled=True)[0, 0]
+    gathered = collect(latents, "mp", 3)[0, 0]
     widened = gathered.astype(jnp.float32)
     average = jnp.mean(widened, axis=-1, keepdims=True)
     centred = widened - average

time: 411 us -> 377 us (0.917)
  waiting for transfers between devices: 284 us -> 219 us
  starting transfers between devices: 5.16 us -> 27.8 us
  local copies, waits for them, and re-layouts: 39.8 us -> 48.4 us
    all_gather x2, waiting for transfers between devices: 53.6 us -> 0.02 us  [gather_seq(): both = lax.all_gather(along, 'c', axis=2)]
    all_gather x1 -> x0, waiting for transfers between devices: 30.5 us -> none  [on_device(): gathered = lax.all_gather(latents, 'mp', axis=3, tiled=True)[0, 0]]
    ppermute x0 -> x7, starting transfers between devices: none -> 22.5 us  [the longest x3 13.7 us: collect(): upper.append(lax.ppermute(upper[-1] if upper else shard, axis, back))]
    ppermute x0 -> x7, waiting for transfers between devices: none -> 14.7 us  [the longest x4 11.6 us: collect(): lower.append(lax.ppermute(lower[-1] if lower else shard, axis, pairs))]
    reduce_scatter x1, waiting for transfers between devices: 40.9 us -> 46 us  [on_device(): lax.psum_scatter(partials.astype(jnp.bfloat16), 'mp', scatter_dimension=1...]
  transfers between devices with their start and end apart: 8 -> 14, of which waited for: 8 -> 9; matrix products, arithmetic and copies ran while one was open for 5% -> 8% of each run, Pallas kernels for 0% -> 0%
where the time goes in v1:
time: 377 us; the launch traced here: 376 us
  waiting for transfers between devices  219 us (58%)
  local copies, waits for them, and re-layouts  48.4 us (13%)
  blocking collectives  45.6 us (12%)
  starting transfers between devices  27.8 us (7%)
  between operations  13.8 us (4%)
  matrix products  12.9 us (3%)
  other arithmetic  7.96 us (2%)
    all_gather x2, waiting for transfers between devices, gather_seq(): along = lax.all_gather(across, 'x', axis=1)  108 us
    reduce_scatter x1, waiting for transfers between devices, on_device(): lax.psum_scatter(partials.astype(jnp.bfloat16), 'mp', scatter_dimension=1...  46 us
    all_gather x1, waiting for transfers between devices, gather_seq(): across = lax.all_gather(block, 'zh', axis=0)  44.4 us
    all_to_all x1, blocking collectives, relay_features(): lax.all_to_all(rows_now, SEQ, split_axis=0, concat_axis=0, tiled=True)  26.1 us
    another operation x1, local copies, waits for them, and re-layouts, on_device(): piece.reshape(height, columns)  21 us
    all_gather x1, blocking collectives, gather_seq(): across = lax.all_gather(block, 'zh', axis=0)  19.6 us
    ppermute x3, starting transfers between devices, collect(): upper.append(lax.ppermute(upper[-1] if upper else shard, axis, back))  13.7 us
    ppermute x4, waiting for transfers between devices, collect(): lower.append(lax.ppermute(lower[-1] if lower else shard, axis, pairs))  11.6 us
  transfers between devices with their start and end apart: 14, of which 9 were waited for; matrix products, arithmetic and copies ran while one was open for 8% of the time, Pallas kernels for 0%

profile of v1, /device:TPU:1, one launch (start us, length us, event | category | flops | bytes accessed | tf_op | source)
XLA Modules:
  0.0 375.8 jit_solution(14466271880126395867)
XLA Ops:
  7.3 19.6 %all-gather.2 = bf16[2,512,256]{2,1,0:T(8,128)(2,1)} all-gather(bf16[1,512,256]{2,1,0:T(8,128)(2,1)} %param.11), channel_id=4, replica_groups=mesh['segment'=4,'zh'=2,'x'=4,'c'=2,'mp'=8] {'zh'}, dimensions={0}, use_global_device_ids=true | all-gather | bytes 786432 | tf_op jit(solution)/shard_map/all_gather | solution.py:67
  26.9 44.4 %all-gather.11.cloned.1.call-done = bf16[2,256,3,512]{3,1,2,0:T(8,128)(2,1)} async-done(((bf16[1,256,3,512]{3,1,2,0:T(8,128)(2,1)}), bf16[2,256,3,512]{3,1,2,0:T(8,128)(2,1)}) %all-gather.11.cloned.1.call-update) | async-done | bytes 1572880 | tf_op jit(solution)/shard_map/all_gather | solution.py:67
  71.4 34.7 %all-gather.17.cloned.1.call-done = bf16[2,2048,256]{2,1,0:T(8,128)(2,1)} async-done(((bf16[2,512,256]{2,1,0:T(8,128)(2,1)}), bf16[2,2048,256]{2,1,0:T(8,128)(2,1)}) %all-gather.17.cloned.1.call-update) | async-done | bytes 2097168 | tf_op jit(solution)/shard_map/all_gather | solution.py:68
  106.2 73.1 %all-gather.13.cloned.1.call-done = bf16[2,1024,3,512]{3,1,2,0:T(8,128)(2,1)} async-done(((bf16[2,256,3,512]{3,1,2,0:T(8,128)(2,1)}), bf16[2,1024,3,512]{3,1,2,0:T(8,128)(2,1)}) %all-gather.13.cloned.1.call-update) | async-done | bytes 6291472 | tf_op jit(solution)/shard_map/all_gather | solution.py:68
  179.3 11.4 %copy.50 = bf16[2,4,256,3,512]{2,1,0,4,3:T(4,128)(2,1)} copy(bf16[2,4,256,3,512]{4,2,1,3,0:T(8,128)(2,1)} %bitcast.128) | data formatting | bytes 12582912 | tf_op jit(solution)/shard_map/all_gather | solution.py:68
  191.7 3.1 collective-permute-start
  194.8 7.0 %collective-permute-done = bf16[1,1,256,512]{3,2,1,0:T(8,128)(2,1)S(1)} collective-permute-done((bf16[1,1,256,512]{3,2,1,0:T(8,128)(2,1)S(1)}, bf16[1,1,256,512]{3,2,1,0:T(8,128)(2,1)S(1)}, u32[]{:S(2)}, u32[]{:S(2)}) %collective-permute-start) | collective-permute-done | bytes 262176 | tf_op jit(solution)/shard_map/ppermute | solution.py:25
  203.7 4.6 %collective-permute-start.4 = (bf16[1,1,256,512]{3,2,1,0:T(8,128)(2,1)S(1)}, bf16[1,1,256,512]{3,2,1,0:T(8,128)(2,1)S(1)}, u32[]{:S(2)}, u32[]{:S(2)}) collective-permute-start(bf16[1,1,256,512]{3,2,1,0:T(8,128)(2,1)S(1)} %copy-done.2), channel_id=1, source_target_pairs={{1,0},{2,1},{3,2},{4,3},{5,4},{6,5},{7,6},{0,7},{9,8},{10,9},{11,1... | collective-permute-start | bytes 786440 | tf_op jit(solution)/shard_map/ppermute | solution.py:27
  208.3 2.8 collective-permute-done.1
  213.0 4.6 %collective-permute-start.5 = (bf16[1,1,256,512]{3,2,1,0:T(8,128)(2,1)S(1)}, bf16[1,1,256,512]{3,2,1,0:T(8,128)(2,1)S(1)}, u32[]{:S(2)}, u32[]{:S(2)}) collective-permute-start(bf16[1,1,256,512]{3,2,1,0:T(8,128)(2,1)S(1)} %collective-permute-done.4), channel_id=1, source_target_pairs={{1,0},{2,1},{3,2},{4,3},{5,4},{6,5},{7,6},{0,7},{9,8},{10,9},{11,1... | collective-permute-start | bytes 786440 | tf_op jit(solution)/shard_map/ppermute | solution.py:27
  223.3 4.6 %collective-permute-start.6 = (bf16[1,1,256,512]{3,2,1,0:T(8,128)(2,1)S(1)}, bf16[1,1,256,512]{3,2,1,0:T(8,128)(2,1)S(1)}, u32[]{:S(2)}, u32[]{:S(2)}) collective-permute-start(bf16[1,1,256,512]{3,2,1,0:T(8,128)(2,1)S(1)} %collective-permute-done.5), channel_id=1, source_target_pairs={{1,0},{2,1},{3,2},{4,3},{5,4},{6,5},{7,6},{0,7},{9,8},{10,9},{11,1... | collective-permute-start | bytes 786440 | tf_op jit(solution)/shard_map/ppermute | solution.py:27
  228.1 3.1 collective-permute-done.6
  232.6 2.8 gather_fusion
  236.5 2.3 fusion.31
  238.8 2.8 copy.49
  241.7 6.4 %copy.52 = bf16[16,256,512]{2,1,0:T(8,128)(2,1)} copy(bf16[16,256,512]{1,2,0:T(8,128)(2,1)} %bitcast.129) | data formatting | bytes 8388608 | tf_op jit(solution)/shard_map/tr,brc->tbc/dot_general | solution.py:123
  248.1 21.0 %reshape_reshape.6 = bf16[4096,1536]{0,1:T(8,128)(2,1)} reshape(bf16[2,4,512,3,512]{2,1,0,4,3:T(4,128)(2,1)} %all-gather.15.cloned.1.call-done) | data formatting | bytes 25165824 | tf_op jit(solution)/shard_map/reshape;reshape | solution.py:99
  269.1 6.6 %convolution_convert_fusion.3 = bf16[256,1536]{1,0:T(8,128)(2,1)S(1)} fusion(bf16[256,4096]{0,1:T(8,128)(2,1)S(1)} %bitcast.132, bf16[4096,1536]{0,1:T(8,128)(2,1)} %reshape_reshape.6), kind=kOutput, calls=%fused_computation.57 | convolution fusion | flops 3221618688 | bytes 15466496 | tf_op jit(solution)/shard_map/dot_general | solution.py:98
  275.7 4.0 %conditional.1 = (bf16[256,512]{0,1:T(8,128)(2,1)S(1)}) conditional(s32[]{:T(128)} %convert_element_type.55, (s32[]{:T(128)}, s32[1,16]{1,0:T(1,128)S(1)}, bf16[256,1536]{1,0:T(8,128)(2,1)S(1)}) %tuple.32, (s32[]{:T(128)}, s32[16]{0:T(128)S(1)}, s32[1,16]{1,0:T(1,128)S(1)}, bf16[256,1536]{1,0:T(8,128)(2,1)S(1)}) %tuple.33), branch_computations={%region_2.5_spmd, %region_5.9_spmd} | conditional | flops 204410160 | bytes 6552408 | solution.py:119
  279.7 4.9 %convolution_convert_fusion.2 = bf16[256,4096]{1,0:T(8,128)(2,1)} fusion(bf16[256,512]{0,1:T(8,128)(2,1)S(1)} %get-tuple-element.44, bf16[4096,512]{1,0:T(8,128)(2,1)} %bitcast.127), kind=kOutput, calls=%fused_computation.49 | convolution fusion | flops 1074790400 | bytes 6553600 | tf_op jit(solution)/shard_map/tr,brc->tbc/dot_general | solution.py:123
  284.6 46.0 %reduce-scatter.2.cloned.1.call-done = bf16[256,512]{1,0:T(8,128)(2,1)} async-done(((bf16[256,4096]{1,0:T(8,128)(2,1)}), bf16[256,512]{1,0:T(8,128)(2,1)}) %reduce-scatter.2.cloned.1.call-update) | async-done | bytes 262160 | tf_op jit(solution)/shard_map/reduce_scatter | solution.py:126
  331.6 26.1 %all_to_all.5 = bf16[16,16,512]{2,1,0:T(8,128)(2,1)S(1)} all-to-all(bf16[16,16,512]{2,1,0:T(8,128)(2,1)S(1)} %bitcast.133), channel_id=1, replica_groups=mesh['segment'=4,'zh'=2,'x'=4,'c'=2,'mp'=8] {'zh','x','c'}, dimensions={0} | all-to-all | bytes 524288 | tf_op jit(solution)/shard_map/all_to_all | solution.py:74
  357.7 5.1 %collective-permute-start.7 = (bf16[16,16,512]{2,1,0:T(8,128)(2,1)S(1)}, bf16[16,16,512]{2,1,0:T(8,128)(2,1)S(1)}, u32[]{:S(2)}, u32[]{:S(2)}) collective-permute-start(bf16[16,16,512]{2,1,0:T(8,128)(2,1)S(1)} %all_to_all.5), channel_id=1, source_target_pairs={{0,128},{128,256},{256,384},{384,0},{1,129},{129,257},{257,385},{3... | collective-permute-start | bytes 786440 | tf_op jit(solution)/shard_map/ppermute | solution.py:36
  362.8 5.5 %collective-permute-done.7 = bf16[16,16,512]{2,1,0:T(8,128)(2,1)S(1)} collective-permute-done((bf16[16,16,512]{2,1,0:T(8,128)(2,1)S(1)}, bf16[16,16,512]{2,1,0:T(8,128)(2,1)S(1)}, u32[]{:S(2)}, u32[]{:S(2)}) %collective-permute-start.7) | collective-permute-done | bytes 262176 | tf_op jit(solution)/shard_map/ppermute | solution.py:36
  (64 shorter events, 19.6 us)
Async XLA Ops:
  6.5 278.1 %copy-start = (f32[1,4096]{1,0:T(1,128)S(1)}, f32[1,4096]{1,0:T(1,128)}, u32[]{:S(2)}) copy-start(f32[1,4096]{1,0:T(1,128)} %param.14) | copy-start | bytes 49156
  6.5 64.8 %all-gather.11.cloned.1.call-start = ((), (), s32[]{:S(2)}) async-start(), calls=%async_computation.2 | async-start | bytes 2359296 | tf_op jit(solution)/shard_map/all_gather | solution.py:67
  7.3 98.9 %all-gather.17.cloned.1.call-start = ((), (), s32[]{:S(2)}) async-start(), calls=%async_computation.6 | async-start | bytes 2621440 | tf_op jit(solution)/shard_map/all_gather | solution.py:68
  26.9 152.4 %all-gather.13.cloned.1.call-start = ((), (), s32[]{:S(2)}) async-start(), calls=%async_computation.4 | async-start | bytes 7864320 | tf_op jit(solution)/shard_map/all_gather | solution.py:68
  71.4 170.3 %all-gather.19.cloned.1.call-start = ((), (), s32[]{:S(2)}) async-start(), calls=%async_computation.7 | async-start | bytes 6291456 | tf_op jit(solution)/shard_map/all_gather | solution.py:69
  106.2 141.9 %all-gather.15.cloned.1.call-start = ((), (), s32[]{:S(2)}) async-start(), calls=%async_computation.5 | async-start | bytes 18874368 | tf_op jit(solution)/shard_map/all_gather | solution.py:69
  190.8 0.9 copy-start.2
  190.8 31.1 %copy-start.3 = (f32[1,4096]{1,0:T(1,128)S(1)}, f32[1,4096]{1,0:T(1,128)}, u32[]{:S(2)}) copy-start(f32[1,4096]{1,0:T(1,128)} %param.12) | copy-start | bytes 49156
  190.8 31.8 %copy-start.4 = (f32[1,4096]{1,0:T(1,128)S(1)}, f32[1,4096]{1,0:T(1,128)}, u32[]{:S(2)}) copy-start(f32[1,4096]{1,0:T(1,128)} %param.13) | copy-start | bytes 49156
  190.8 139.8 %reduce-scatter.2.cloned.1.call-start = ((), (), s32[]{:S(2)}) async-start(), calls=%async_computation.3 | async-start | bytes 2359296 | tf_op jit(solution)/shard_map/reduce_scatter | solution.py:126
  191.7 10.1 %collective-permute-start = (bf16[1,1,256,512]{3,2,1,0:T(8,128)(2,1)S(1)}, bf16[1,1,256,512]{3,2,1,0:T(8,128)(2,1)S(1)}, u32[]{:S(2)}, u32[]{:S(2)}) collective-permute-start(bf16[1,1,256,512]{3,2,1,0:T(8,128)(2,1)S(1)} %copy-done.2), channel_id=1, source_target_pairs={{0,1},{1,2},{2,3},{3,4},{4,5},{5,6},{6,7},{7,0},{8,9},{9,10},{10,1... | collective-permute-start | bytes 786440 | tf_op jit(solution)/shard_map/ppermute | solution.py:25
  201.8 9.3 %collective-permute-start.1 = (bf16[1,1,256,512]{3,2,1,0:T(8,128)(2,1)S(1)}, bf16[1,1,256,512]{3,2,1,0:T(8,128)(2,1)S(1)}, u32[]{:S(2)}, u32[]{:S(2)}) collective-permute-start(bf16[1,1,256,512]{3,2,1,0:T(8,128)(2,1)S(1)} %collective-permute-done), channel_id=1, source_target_pairs={{0,1},{1,2},{2,3},{3,4},{4,5},{5,6},{6,7},{7,0},{8,9},{9,10},{10,1... | collective-permute-start | bytes 786440 | tf_op jit(solution)/shard_map/ppermute | solution.py:25
  203.7 9.3 %collective-permute-start.4 = (bf16[1,1,256,512]{3,2,1,0:T(8,128)(2,1)S(1)}, bf16[1,1,256,512]{3,2,1,0:T(8,128)(2,1)S(1)}, u32[]{:S(2)}, u32[]{:S(2)}) collective-permute-start(bf16[1,1,256,512]{3,2,1,0:T(8,128)(2,1)S(1)} %copy-done.2), channel_id=1, source_target_pairs={{1,0},{2,1},{3,2},{4,3},{5,4},{6,5},{7,6},{0,7},{9,8},{10,9},{11,1... | collective-permute-start | bytes 786440 | tf_op jit(solution)/shard_map/ppermute | solution.py:27
  211.1 8.3 %collective-permute-start.2 = (bf16[1,1,256,512]{3,2,1,0:T(8,128)(2,1)S(1)}, bf16[1,1,256,512]{3,2,1,0:T(8,128)(2,1)S(1)}, u32[]{:S(2)}, u32[]{:S(2)}) collective-permute-start(bf16[1,1,256,512]{3,2,1,0:T(8,128)(2,1)S(1)} %collective-permute-done.1), channel_id=1, source_target_pairs={{0,1},{1,2},{2,3},{3,4},{4,5},{5,6},{6,7},{7,0},{8,9},{9,10},{10,1... | collective-permute-start | bytes 786440 | tf_op jit(solution)/shard_map/ppermute | solution.py:25
  213.0 10.3 %collective-permute-start.5 = (bf16[1,1,256,512]{3,2,1,0:T(8,128)(2,1)S(1)}, bf16[1,1,256,512]{3,2,1,0:T(8,128)(2,1)S(1)}, u32[]{:S(2)}, u32[]{:S(2)}) collective-permute-start(bf16[1,1,256,512]{3,2,1,0:T(8,128)(2,1)S(1)} %collective-permute-done.4), channel_id=1, source_target_pairs={{1,0},{2,1},{3,2},{4,3},{5,4},{6,5},{7,6},{0,7},{9,8},{10,9},{11,1... | collective-permute-start | bytes 786440 | tf_op jit(solution)/shard_map/ppermute | solution.py:27
  219.4 8.5 %collective-permute-start.3 = (bf16[1,1,256,512]{3,2,1,0:T(8,128)(2,1)S(1)}, bf16[1,1,256,512]{3,2,1,0:T(8,128)(2,1)S(1)}, u32[]{:S(2)}, u32[]{:S(2)}) collective-permute-start(bf16[1,1,256,512]{3,2,1,0:T(8,128)(2,1)S(1)} %collective-permute-done.2), channel_id=1, source_target_pairs={{0,1},{1,2},{2,3},{3,4},{4,5},{5,6},{6,7},{7,0},{8,9},{9,10},{10,1... | collective-permute-start | bytes 786440 | tf_op jit(solution)/shard_map/ppermute | solution.py:25
  223.3 7.9 %collective-permute-start.6 = (bf16[1,1,256,512]{3,2,1,0:T(8,128)(2,1)S(1)}, bf16[1,1,256,512]{3,2,1,0:T(8,128)(2,1)S(1)}, u32[]{:S(2)}, u32[]{:S(2)}) collective-permute-start(bf16[1,1,256,512]{3,2,1,0:T(8,128)(2,1)S(1)} %collective-permute-done.5), channel_id=1, source_target_pairs={{1,0},{2,1},{3,2},{4,3},{5,4},{6,5},{7,6},{0,7},{9,8},{10,9},{11,1... | collective-permute-start | bytes 786440 | tf_op jit(solution)/shard_map/ppermute | solution.py:27
  231.2 1.4 copy-start.1
  269.1 6.6 %copy-start.5 = (s32[1,16]{1,0:T(1,128)S(1)}, s32[1,16]{1,0:T(1,128)}, u32[]{:S(2)}) copy-start(s32[1,16]{1,0:T(1,128)} %param.15) | copy-start | bytes 196
  357.7 10.6 %collective-permute-start.7 = (bf16[16,16,512]{2,1,0:T(8,128)(2,1)S(1)}, bf16[16,16,512]{2,1,0:T(8,128)(2,1)S(1)}, u32[]{:S(2)}, u32[]{:S(2)}) collective-permute-start(bf16[16,16,512]{2,1,0:T(8,128)(2,1)S(1)} %all_to_all.5), channel_id=1, source_target_pairs={{0,128},{128,256},{256,384},{384,0},{1,129},{129,257},{257,385},{3... | collective-permute-start | bytes 786440 | tf_op jit(solution)/shard_map/ppermute | solution.py:36
Sparse Core Ops, SparseCore 0:
  9.4 61.9 all-gather.10
  73.5 32.6 all-gather.16
  108.2 71.0 all-gather.12
  181.3 24.1 all-gather.18
  207.4 34.0 all-gather.14
  284.7 45.8 reduce-scatter.1
